TPU v7x, 128 devices: a whole 4x4x4 slice. The times are simulated.
128 devices in a mesh: inp: 8 (over z_lo, y), wide: 16 (over z_hi, x, core).
Axes of the slice: x: 4, y: 4, z: 4 (z_hi: 2, z_lo: 2; z = z_hi * 2 + z_lo), core: 2. Of those that a mesh axis runs over, the one named last changes fastest.
Arguments:
- voltages: int32 [1280, 196608], P('inp', 'wide'), may hold values from -8 to 7
- prototype: float32 [4, 4096], replicated, may hold values from -0.75 to 0.75
- input_gain: float32 [1280], P('inp'), may hold values from 0.5 to 1.5
- usable: int32 [1280], P('inp'), may hold values 0 or 1
Outputs:
- visibility: float32 [2, 128, 1280, 1280], P(None, 'wide', 'inp')
All inputs are finite; a program needn't handle non-finite values. No bound on the sum of `usable` on one device may be relied on, other than what follows from the above.
Results may differ from a plain program's by a relative error of at most 0.0035.
Values may be sent and summed in bfloat16 or wider, within the bound.
No kernel may reach another device: no remote copies, remote signals or barrier semaphores. Data moves between devices by JAX's collectives and lax.ppermute only.
A program may use at most 192 MiB of HBM per device.

v0:
```python
import math

import jax
import jax.numpy as jnp
from jax import lax
from jax.sharding import PartitionSpec as P

AVG = 16


def passed_along(value, axis, steps):
    count = lax.axis_size(axis)
    initial, last = (max(0, -steps), min(count, count - steps))
    return lax.ppermute(value, axis, [(source, source + steps) for source in range(initial, last)])


def phase_tables(rows_count, cols_count, modulus):
    first_index = jnp.arange(rows_count, dtype=jnp.int32)[:, None]
    second_index = jnp.arange(cols_count, dtype=jnp.int32)[None, :]
    angle = (first_index * second_index % modulus).astype(jnp.float32) * (2.0 * math.pi / modulus)
    return (jnp.cos(angle), jnp.sin(angle))


def transform(filtered, channels):
    total_rows, span_len = filtered.shape
    inner_len = min(span_len, 128)
    outer_len = span_len // inner_len
    kept_count = channels // outer_len
    highest = lax.Precision.HIGHEST
    reshaped = filtered.reshape(total_rows, outer_len, inner_len)
    cos_one, sin_one = phase_tables(outer_len, outer_len, outer_len)
    section_real = jnp.einsum("ran,ak->rkn", reshaped, cos_one, precision=highest)
    section_imag = -jnp.einsum("ran,ak->rkn", reshaped, sin_one, precision=highest)
    cos_two, sin_two = phase_tables(outer_len, inner_len, span_len)
    turned_real = section_real * cos_two + section_imag * sin_two
    turned_imag = section_imag * cos_two - section_real * sin_two
    cos_three, sin_three = phase_tables(inner_len, kept_count, inner_len)
    real_out = jnp.einsum("rkn,nm->rmk", turned_real, cos_three, precision=highest) + jnp.einsum(
        "rkn,nm->rmk", turned_imag, sin_three, precision=highest
    )
    imag_out = jnp.einsum("rkn,nm->rmk", turned_imag, cos_three, precision=highest) - jnp.einsum(
        "rkn,nm->rmk", turned_real, sin_three, precision=highest
    )
    return (real_out.reshape(total_rows, channels), imag_out.reshape(total_rows, channels))


def shards(voltages, prototype, input_gain, usable):
    members, width_all = voltages.shape
    taps_count, span_len = prototype.shape
    frames_own = width_all // span_len
    channels = span_len // 2
    samples = voltages.astype(jnp.float32).reshape(members, frames_own, span_len)
    near_sum = jnp.zeros(samples.shape, jnp.float32)
    for tap_index in range(taps_count):
        delayed = jnp.pad(samples[:, : frames_own - tap_index], ((0, 0), (tap_index, 0), (0, 0)))
        near_sum = near_sum + prototype[tap_index][None, None, :] * delayed
    edge_parts = []
    for frame_index in range(taps_count - 1):
        partial_sum = jnp.zeros((members, span_len), jnp.float32)
        for tap_index in range(frame_index + 1, taps_count):
            partial_sum = (
                partial_sum
                + prototype[tap_index][None, :] * samples[:, frames_own + frame_index - tap_index]
            )
        edge_parts.append(partial_sum)
    outgoing = jnp.stack(edge_parts, axis=1).astype(jnp.bfloat16)
    incoming = passed_along(outgoing, "wide", 1).astype(jnp.float32)
    filtered = jnp.concatenate([near_sum + incoming, near_sum[:, taps_count - 1 :]], axis=1)
    real_out, imag_out = transform(filtered.reshape(members * frames_own, span_len), channels)
    factor = (input_gain * usable.astype(jnp.float32) / math.sqrt(span_len))[:, None, None]
    spectra = jnp.stack(
        [
            real_out.reshape(members, frames_own, channels) * factor,
            imag_out.reshape(members, frames_own, channels) * factor,
        ]
    ).astype(jnp.bfloat16)
    arrived = lax.all_to_all(spectra, "wide", split_axis=3, concat_axis=2, tiled=True)
    frames_all = arrived.shape[2]
    chan_own = arrived.shape[3]
    group_count = chan_own // AVG
    own_spectra = arrived.reshape(2, members, frames_all, group_count, AVG)
    normalize = 1.0 / math.sqrt(AVG * frames_all)
    fetched = lax.all_gather(arrived, "inp", axis=1, tiled=True)
    others = fetched.reshape(2, fetched.shape[1], frames_all, group_count, AVG)
    products = jnp.einsum(
        "pafgc,qbfgc->pqgab", own_spectra, others, preferred_element_type=jnp.float32
    )
    return jnp.stack([products[0, 0] + products[1, 1], products[1, 0] - products[0, 1]]) * normalize


def solution(mesh):
    return jax.shard_map(
        shards,
        mesh=mesh,
        in_specs=(P("inp", "wide"), P(), P("inp"), P("inp")),
        out_specs=P(None, "wide", "inp", None),
        check_vma=False,
    )
```

profile of v0, /device:TPU:0, one launch (start us, length us, event | category | flops | bytes accessed | tf_op | source)
XLA Modules:
  0.0 775.1 jit_solution(13533302733139891966)
XLA Ops:
  6.5 0.0 all-gather.2.cloned.1.call-start
  6.5 1.1 fusion.83
  7.6 3.9 convert_element_type.49
  11.5 0.9 copy.114
  12.4 1.2 add_convert_fusion.1
  13.6 0.5 pad_maximum_fusion.1
  14.1 0.0 copy-start.2
  14.1 0.0 copy-start.3
  14.1 3.4 collective-permute-start
  17.6 0.6 slice.58
  18.2 0.1 fusion.55
  18.3 0.0 copy-done.2
  18.3 0.0 copy-done.3
  18.3 3.6 collective-permute-done
  21.9 5.8 convert_add_fusion
  27.7 12.7 %copy.64 = f32[160,3,4096]{2,1,0:T(4,128)} copy(f32[160,3,4096]{2,0,1:T(8,128)} %convert_add_fusion) | data formatting | bytes 15728640 | tf_op jit(solution)/shard_map/add | solution.py:68
  40.4 13.6 %reshape_reshape.9 = f32[480,32,128]{2,1,0:T(8,128)} reshape(f32[160,3,4096]{2,1,0:T(4,128)} %copy.64) | data formatting | bytes 15728640 | tf_op jit(solution)/shard_map/reshape;reshape | solution.py:30
  54.0 0.0 copy-start
  54.0 11.7 %fusion.37 = f32[32,480,128]{2,0,1:T(8,128)} fusion(f32[480,32,128]{2,1,0:T(8,128)} %reshape_reshape.9), kind=kOutput, calls=%fused_computation.57 | convolution fusion | flops 754989056 | bytes 15728640 | tf_op jit(solution)/shard_map/ran,ak->rkn/dot_general | solution.py:33
  65.8 0.0 copy-done
  65.8 12.4 %add_bitcast_fusion = (f32[480,32,128]{2,1,0:T(8,128)S(1)}, f32[480,32,128]{2,1,0:T(8,128)}) fusion(f32[32,480,128]{2,0,1:T(8,128)} %fusion.37, f32[32,128]{1,0:T(8,128)S(1)} %get-tuple-element.17, f32[32,128]{1,0:T(8,128)S(1)} %get-tuple-element.18, f32[480,32,128]{2,1,0:T(8,128)S(1)} %copy-done), kind=kOutput, calls=%fused_computation.6 | convolution fusion | flops 768751616 | bytes 31490048 | tf_op jit(solution)/shard_map/ran,ak->rkn/dot_general | solution.py:32
  78.1 0.0 copy-start.1
  78.1 15.4 %fusion.5 = f32[64,480,32]{1,0,2:T(8,128)S(1)} fusion(f32[480,32,128]{2,1,0:T(8,128)} %get-tuple-element.6), kind=kOutput, calls=%fused_computation.8 | convolution fusion | flops 1510064128 | bytes 11796480 | tf_op jit(solution)/shard_map/rkn,nm->rmk/dot_general | solution.py:41
  93.5 0.0 copy-done.1
  93.5 14.5 %fusion.7 = f32[64,480,32]{1,0,2:T(8,128)S(1)} fusion(f32[480,32,128]{2,1,0:T(8,128)S(1)} %copy-done.1), kind=kOutput, calls=%fused_computation.10 | convolution fusion | flops 1510064128 | bytes 11796480 | tf_op jit(solution)/shard_map/rkn,nm->rmk/dot_general | solution.py:38
  108.1 17.9 %add_bitcast_fusion.1 = f32[480,64,32]{0,1,2:T(8,128)} fusion(f32[64,480,32]{1,0,2:T(8,128)S(1)} %fusion.7, f32[480,32,128]{2,1,0:T(8,128)S(1)} %get-tuple-element.5), kind=kOutput, calls=%fused_computation.27 | convolution fusion | flops 1511047168 | bytes 15728640 | tf_op jit(solution)/shard_map/rkn,nm->rmk/dot_general | solution.py:38
  125.9 18.1 %subtract_bitcast_fusion.1 = f32[480,64,32]{0,1,2:T(8,128)} fusion(f32[64,480,32]{1,0,2:T(8,128)S(1)} %fusion.5, f32[480,32,128]{2,1,0:T(8,128)S(1)} %get-tuple-element.5), kind=kOutput, calls=%fused_computation.26 | convolution fusion | flops 1511047168 | bytes 15728640 | tf_op jit(solution)/shard_map/rkn,nm->rmk/dot_general | solution.py:41
  144.0 10.6 %copy.70 = f32[480,64,32]{2,1,0:T(8,128)} copy(f32[480,64,32]{0,1,2:T(8,128)} %subtract_bitcast_fusion.1) | data formatting | bytes 7864320 | tf_op jit(solution)/shard_map/sub | solution.py:41
  154.6 15.0 %reshape_reshape.11 = f32[1,160,3,2048]{3,2,1,0:T(4,128)} reshape(f32[480,64,32]{2,1,0:T(8,128)} %copy.70) | data formatting | bytes 7864320 | tf_op jit(solution)/shard_map/reshape;reshape | solution.py:74
  169.6 10.6 %copy.67 = f32[480,64,32]{2,1,0:T(8,128)} copy(f32[480,64,32]{0,1,2:T(8,128)} %add_bitcast_fusion.1) | data formatting | bytes 7864320 | tf_op jit(solution)/shard_map/add | solution.py:38
  180.3 15.3 %reshape_reshape.10 = f32[1,160,3,2048]{3,2,1,0:T(4,128)} reshape(f32[480,64,32]{2,1,0:T(8,128)} %copy.67) | data formatting | bytes 7864320 | tf_op jit(solution)/shard_map/reshape;reshape | solution.py:73
  195.6 7.3 multiply_convert_fusion.1
  202.9 6.1 pad_maximum_fusion
  209.0 21.6 %copy.71 = bf16[2,160,3,2048]{1,0,2,3:T(2,128)(2,1)} copy(bf16[2,160,3,2048]{3,2,1,0:T(4,128)(2,1)} %pad_maximum_fusion) | data formatting | bytes 7864320 | tf_op jit(solution)/shard_map/stack | solution.py:71
  230.6 122.8 %all_to_all.18 = bf16[2,160,3,2048]{1,0,2,3:T(2,128)(2,1)} all-to-all(bf16[2,160,3,2048]{1,0,2,3:T(2,128)(2,1)} %copy.71), channel_id=1, replica_groups=mesh['inp'=8,'wide'=16] {'wide'}, dimensions={3} | all-to-all | bytes 7864320 | tf_op jit(solution)/shard_map/all_to_all | solution.py:77
  353.4 15.7 %copy.84 = bf16[2,160,3,16,128]{4,1,2,3,0:T(8,128)(2,1)} copy(bf16[2,160,3,16,128]{1,0,2,4,3:T(2,128)(2,1)} %bitcast.72) | data formatting | bytes 7864320 | tf_op jit(solution)/shard_map/all_to_all | solution.py:77
  369.0 0.0 all-gather.2.cloned.1.call-update
  369.1 7.0 copy.87
  376.0 298.3 %all-gather.2.cloned.1.call-done = bf16[2,1280,48,128]{3,1,2,0:T(8,128)(2,1)} async-done(((bf16[2,160,48,128]{3,1,2,0:T(8,128)(2,1)}), bf16[2,1280,48,128]{3,1,2,0:T(8,128)(2,1)}) %all-gather.2.cloned.1.call-update) | async-done | bytes 31457296 | tf_op jit(solution)/shard_map/all_gather | solution.py:83
  674.4 41.1 %copy.74 = bf16[2,1280,48,128]{1,3,2,0:T(8,128)(2,1)} copy(bf16[2,1280,48,128]{3,1,2,0:T(8,128)(2,1)} %all-gather.2.cloned.1.call-done) | data formatting | bytes 62914560 | tf_op jit(solution)/shard_map/all_gather | solution.py:83
  715.4 24.5 %fusion.2 = f32[2,2,8,160,1280]{4,3,0,1,2:T(8,128)} fusion(bf16[2,1280,48,8,16,1]{1,4,3,2,0,5:T(8,128)(2,1)} %bitcast.76, bf16[2,160,48,8,16,1]{1,4,3,2,0,5:T(8,128)(2,1)} %bitcast.78), kind=kOutput, calls=%fused_computation.2 | convolution fusion | flops 10066329600 | bytes 61603840 | tf_op jit(solution)/shard_map/pafgc,qbfgc->pqgab/dot_general | solution.py:85
  740.0 8.4 %fusion.13 = f32[1,8,160,1280]{3,2,1,0:T(8,128)} fusion(f32[2,2,8,160,1280]{4,3,0,1,2:T(8,128)} %fusion.2), kind=kLoop, calls=%fused_computation.17 | loop fusion | flops 1638400 | bytes 19660800 | tf_op jit(solution)/shard_map/sub | solution.py:88
  748.4 8.3 %fusion.15 = f32[1,8,160,1280]{3,2,1,0:T(8,128)} fusion(f32[2,2,8,160,1280]{4,3,0,1,2:T(8,128)} %fusion.2), kind=kLoop, calls=%fused_computation.20 | loop fusion | flops 1638400 | bytes 19660800 | tf_op jit(solution)/shard_map/add | solution.py:88
  756.7 11.0 %maximum_multiply_fusion = f32[2,8,160,1280]{3,2,1,0:T(8,128)} fusion(f32[1,8,160,1280]{3,2,1,0:T(8,128)} %fusion.13, f32[1,8,160,1280]{3,2,1,0:T(8,128)} %fusion.15), kind=kLoop, calls=%fused_computation.3 | loop fusion | flops 6553600 | bytes 26214400 | tf_op jit(solution)/shard_map/mul | solution.py:88
  (2 shorter events, 0.0 us)
Async XLA Ops:
  6.5 667.8 %all-gather.2.cloned.1.call-start = ((), (), s32[]{:S(2)}) async-start(), calls=%async_computation.1 | async-start | bytes 35389440 | tf_op jit(solution)/shard_map/all_gather | solution.py:83
  14.1 4.2 copy-start.2
  14.1 4.2 copy-start.3
  14.1 7.8 %collective-permute-start = (bf16[160,3,4096]{2,0,1:T(8,128)(2,1)S(1)}, bf16[160,3,4096]{2,0,1:T(8,128)(2,1)}, u32[]{:S(2)}, u32[]{:S(2)}) collective-permute-start(bf16[160,3,4096]{2,0,1:T(8,128)(2,1)S(1)} %pad_maximum_fusion.1), channel_id=1, source_target_pairs={{0,1},{1,2},{2,3},{3,4},{4,5},{5,6},{6,7},{7,8},{8,9},{9,10},{10,1... | collective-permute-start | bytes 11796488 | tf_op jit(solution)/shard_map/ppermute | solution.py:14
  54.0 11.7 %copy-start = (f32[480,32,128]{2,1,0:T(8,128)S(1)}, f32[480,32,128]{2,1,0:T(8,128)}, u32[]{:S(2)}) copy-start(f32[480,32,128]{2,1,0:T(8,128)} %reshape_reshape.9) | copy-start | bytes 23592964
  78.1 15.4 %copy-start.1 = (f32[480,32,128]{2,1,0:T(8,128)S(1)}, f32[480,32,128]{2,1,0:T(8,128)}, u32[]{:S(2)}) copy-start(f32[480,32,128]{2,1,0:T(8,128)} %get-tuple-element.6) | copy-start | bytes 23592964
Sparse Core Ops, SparseCore 0:
  369.2 305.1 all-gather.1
where the time goes:
time: 782 us; the launch traced here: 775 us
  waiting for transfers between devices  302 us (39%)
  local copies, waits for them, and re-layouts  166 us (21%)
  blocking collectives  123 us (16%)
  matrix products  114 us (15%)
  other arithmetic  52.6 us (7%)
  between operations  14 us (2%)
    all_gather x1, waiting for transfers between devices, shards(): fetched = lax.all_gather(arrived, 'inp', axis=1, tiled=True)  298 us
    all_to_all x1, blocking collectives, shards(): lax.all_to_all(spectra, 'wide', split_axis=3, concat_axis=2, tiled=True)  123 us
    all_gather x1, local copies, waits for them, and re-layouts, shards(): fetched = lax.all_gather(arrived, 'inp', axis=1, tiled=True)  41.1 us
    dot_general x1, matrix products, shards(): jnp.einsum('pafgc,qbfgc->pqgab', own_spectra, others, preferred_element_t...  24.5 us
    all_to_all x2, local copies, waits for them, and re-layouts, shards(): lax.all_to_all(spectra, 'wide', split_axis=3, concat_axis=2, tiled=True)  22.6 us
    another operation x1, local copies, waits for them, and re-layouts, shards(): jnp.stack([real_out.reshape(members, frames_own, channels) * factor, imag...  21.6 us
    dot_general x1, matrix products, transform(): jnp.einsum('rkn,nm->rmk', turned_real, sin_three, precision=highest)  18.1 us
    dot_general x1, matrix products, transform(): jnp.einsum('rkn,nm->rmk', turned_real, cos_three, precision=highest)  17.9 us
  transfers between devices with their start and end apart: 2, of which 2 were waited for; matrix products, arithmetic and copies ran while one was open for 1% of the time, Pallas kernels for 0%

commit v1 on v0

--- a/solution.py
+++ b/solution.py
@@ -44,7 +44,7 @@
     return (real_out.reshape(total_rows, channels), imag_out.reshape(total_rows, channels))
 
 
-def shards(voltages, prototype, input_gain, usable):
+def channelize(voltages, prototype, input_gain, usable):
     members, width_all = voltages.shape
     taps_count, span_len = prototype.shape
     frames_own = width_all // span_len
@@ -68,24 +68,35 @@
     filtered = jnp.concatenate([near_sum + incoming, near_sum[:, taps_count - 1 :]], axis=1)
     real_out, imag_out = transform(filtered.reshape(members * frames_own, span_len), channels)
     factor = (input_gain * usable.astype(jnp.float32) / math.sqrt(span_len))[:, None, None]
-    spectra = jnp.stack(
+    return jnp.stack(
         [
             real_out.reshape(members, frames_own, channels) * factor,
             imag_out.reshape(members, frames_own, channels) * factor,
         ]
     ).astype(jnp.bfloat16)
-    arrived = lax.all_to_all(spectra, "wide", split_axis=3, concat_axis=2, tiled=True)
-    frames_all = arrived.shape[2]
-    chan_own = arrived.shape[3]
-    group_count = chan_own // AVG
-    own_spectra = arrived.reshape(2, members, frames_all, group_count, AVG)
-    normalize = 1.0 / math.sqrt(AVG * frames_all)
-    fetched = lax.all_gather(arrived, "inp", axis=1, tiled=True)
-    others = fetched.reshape(2, fetched.shape[1], frames_all, group_count, AVG)
-    products = jnp.einsum(
-        "pafgc,qbfgc->pqgab", own_spectra, others, preferred_element_type=jnp.float32
+
+
+def shards(voltages, prototype, input_gain, usable):
+    spectra = channelize(voltages, prototype, input_gain, usable)
+    _, members, frames_own, channels = spectra.shape
+    n_inp = lax.axis_size("inp")
+    n_wide = lax.axis_size("wide")
+    n_dev = n_inp * n_wide
+    group_width = channels // n_dev
+    chunks = spectra.reshape(2, members, frames_own, n_dev, group_width).transpose(3, 0, 1, 2, 4)
+    arrived = lax.all_to_all(chunks, ("wide", "inp"), 0, 0, tiled=True)
+    arrived = arrived.reshape(n_wide, n_inp, 2, members, frames_own, group_width)
+    every = arrived.transpose(2, 1, 3, 0, 4, 5).reshape(2, n_inp * members, n_wide * frames_own * group_width)
+    real_part, imag_part = every[0], every[1]
+    left = jnp.stack(
+        [jnp.concatenate([real_part, imag_part], axis=1), jnp.concatenate([imag_part, -real_part], axis=1)]
     )
-    return jnp.stack([products[0, 0] + products[1, 1], products[1, 0] - products[0, 1]]) * normalize
+    right = jnp.concatenate([real_part, imag_part], axis=1)
+    normalize = 1.0 / math.sqrt(n_wide * frames_own * AVG)
+    left = left.reshape(2, n_inp, members, left.shape[-1])
+    products = jnp.einsum("pjak,bk->jpab", left, right, preferred_element_type=jnp.float32) * normalize
+    spread = lax.all_to_all(products, "inp", 0, 0, tiled=True)
+    return spread.transpose(1, 0, 2, 3)
 
 
 def solution(mesh):

time: 782 us -> 656 us (0.84)
  waiting for transfers between devices: 302 us -> 3.62 us
  blocking collectives: 123 us -> 279 us
  local copies, waits for them, and re-layouts: 166 us -> 190 us
  between operations: 14 us -> 0.61 us
  other arithmetic: 52.6 us -> 65.6 us
    all_gather x1 -> x0, waiting for transfers between devices: 298 us -> none  [shards(): fetched = lax.all_gather(arrived, 'inp', axis=1, tiled=True)]
    all_to_all x1 -> x2, blocking collectives: 123 us -> 279 us  [the longest x1 152 us: shards(): spread = lax.all_to_all(products, 'inp', 0, 0, tiled=True)]
    transpose x0 -> x2, local copies, waits for them, and re-layouts: none -> 46.3 us  [the longest x1 35.3 us: shards(): spectra.reshape(2, members, frames_own, n_dev, group_width)]
    all_gather x1 -> x0, local copies, waits for them, and re-layouts: 41.1 us -> none  [shards(): fetched = lax.all_gather(arrived, 'inp', axis=1, tiled=True)]
    all_to_all x2 -> x0, local copies, waits for them, and re-layouts: 22.6 us -> none  [shards(): lax.all_to_all(spectra, 'wide', split_axis=3, concat_axis=2, tiled=True)]
    transpose x0 -> x1, other arithmetic: none -> 21.6 us  [shards(): spectra.reshape(2, members, frames_own, n_dev, group_width)]
    squeeze x0 -> x4, local copies, waits for them, and re-layouts: none -> 20.6 us  [shards(): real_part, imag_part = (every[0], every[1])]
    another operation x4 -> x3, other arithmetic: 15 us -> 32.4 us
  transfers between devices with their start and end apart: 2 -> 1, of which waited for: 2 -> 1; matrix products, arithmetic and copies ran while one was open for 1% -> 0% of each run, Pallas kernels for 0% -> 0%
where the time goes in v1:
time: 656 us; the launch traced here: 648 us
  blocking collectives  279 us (43%)
  local copies, waits for them, and re-layouts  190 us (29%)
  matrix products  107 us (16%)
  other arithmetic  65.6 us (10%)
    all_to_all x1, blocking collectives, shards(): spread = lax.all_to_all(products, 'inp', 0, 0, tiled=True)  152 us
    all_to_all x1, blocking collectives, shards(): arrived = lax.all_to_all(chunks, ('wide', 'inp'), 0, 0, tiled=True)  127 us
    transpose x1, local copies, waits for them, and re-layouts, shards(): spectra.reshape(2, members, frames_own, n_dev, group_width)  35.3 us
    another operation x2, other arithmetic  31.9 us
    another operation x1, local copies, waits for them, and re-layouts, channelize(): real_out.reshape(members, frames_own, channels) * factor  23 us
    another operation x1, local copies, waits for them, and re-layouts, channelize(): imag_out.reshape(members, frames_own, channels) * factor  23 us
    transpose x1, other arithmetic, shards(): spectra.reshape(2, members, frames_own, n_dev, group_width)  21.6 us
    squeeze x4, local copies, waits for them, and re-layouts, shards(): real_part, imag_part = (every[0], every[1])  20.6 us
  transfers between devices with their start and end apart: 1, of which 1 were waited for; matrix products, arithmetic and copies ran while one was open for 0% of the time, Pallas kernels for 0%

profile of v1, /device:TPU:0, one launch (start us, length us, event | category | flops | bytes accessed | tf_op | source)
XLA Modules:
  0.0 648.5 jit_solution(9485092023332894730)
XLA Ops:
  0.0 1.1 fusion.85
  1.1 3.9 convert_element_type.50
  4.9 0.9 copy.112
  5.8 1.2 add_convert_fusion.1
  7.0 0.0 copy-start.2
  7.0 0.0 copy-start.3
  7.0 0.5 pad_maximum_fusion
  7.5 3.5 collective-permute-start
  11.0 0.6 slice.52
  11.6 0.1 fusion.55
  11.7 0.0 copy-done.2
  11.7 0.0 copy-done.3
  11.7 3.6 collective-permute-done
  15.3 5.7 convert_add_fusion
  21.1 12.7 %copy.75 = f32[160,3,4096]{2,1,0:T(4,128)} copy(f32[160,3,4096]{2,0,1:T(8,128)} %convert_add_fusion) | data formatting | bytes 15728640 | tf_op jit(solution)/shard_map/add | solution.py:68
  33.8 13.6 %reshape_reshape.9 = f32[480,32,128]{2,1,0:T(8,128)} reshape(f32[160,3,4096]{2,1,0:T(4,128)} %copy.75) | data formatting | bytes 15728640 | tf_op jit(solution)/shard_map/reshape;reshape | solution.py:30
  47.3 0.0 copy-start
  47.3 11.8 %fusion.37 = f32[32,480,128]{2,0,1:T(8,128)} fusion(f32[480,32,128]{2,1,0:T(8,128)} %reshape_reshape.9), kind=kOutput, calls=%fused_computation.57 | convolution fusion | flops 754989056 | bytes 15728640 | tf_op jit(solution)/shard_map/ran,ak->rkn/dot_general | solution.py:33
  59.2 0.0 copy-done
  59.2 12.4 %add_bitcast_fusion = (f32[480,32,128]{2,1,0:T(8,128)S(1)}, f32[480,32,128]{2,1,0:T(8,128)}) fusion(f32[32,480,128]{2,0,1:T(8,128)} %fusion.37, f32[32,128]{1,0:T(8,128)S(1)} %get-tuple-element.19, f32[32,128]{1,0:T(8,128)S(1)} %get-tuple-element.20, f32[480,32,128]{2,1,0:T(8,128)S(1)} %copy-done), kind=kOutput, calls=%fused_computation.13 | convolution fusion | flops 768751616 | bytes 31490048 | tf_op jit(solution)/shard_map/ran,ak->rkn/dot_general | solution.py:32
  71.5 0.0 copy-start.1
  71.5 15.4 %fusion.7 = f32[64,480,32]{1,0,2:T(8,128)S(1)} fusion(f32[480,32,128]{2,1,0:T(8,128)} %get-tuple-element.6), kind=kOutput, calls=%fused_computation.15 | convolution fusion | flops 1510064128 | bytes 11796480 | tf_op jit(solution)/shard_map/rkn,nm->rmk/dot_general | solution.py:41
  86.9 0.0 copy-done.1
  86.9 14.5 %fusion.9 = f32[64,480,32]{1,0,2:T(8,128)S(1)} fusion(f32[480,32,128]{2,1,0:T(8,128)S(1)} %copy-done.1), kind=kOutput, calls=%fused_computation.17 | convolution fusion | flops 1510064128 | bytes 11796480 | tf_op jit(solution)/shard_map/rkn,nm->rmk/dot_general | solution.py:38
  101.4 17.9 %add_bitcast_fusion.1 = f32[480,64,32]{0,1,2:T(8,128)} fusion(f32[64,480,32]{1,0,2:T(8,128)S(1)} %fusion.9, f32[480,32,128]{2,1,0:T(8,128)S(1)} %get-tuple-element.5), kind=kOutput, calls=%fused_computation.24 | convolution fusion | flops 1511047168 | bytes 15728640 | tf_op jit(solution)/shard_map/rkn,nm->rmk/dot_general | solution.py:38
  119.3 18.1 %subtract_bitcast_fusion.1 = f32[480,64,32]{0,1,2:T(8,128)} fusion(f32[64,480,32]{1,0,2:T(8,128)S(1)} %fusion.7, f32[480,32,128]{2,1,0:T(8,128)S(1)} %get-tuple-element.5), kind=kOutput, calls=%fused_computation.23 | convolution fusion | flops 1511047168 | bytes 15728640 | tf_op jit(solution)/shard_map/rkn,nm->rmk/dot_general | solution.py:41
  137.4 10.8 %copy.81 = f32[480,64,32]{2,1,0:T(8,128)} copy(f32[480,64,32]{0,1,2:T(8,128)} %subtract_bitcast_fusion.1) | data formatting | bytes 7864320 | tf_op jit(solution)/shard_map/sub | solution.py:41
  148.1 10.6 %copy.78 = f32[480,64,32]{2,1,0:T(8,128)} copy(f32[480,64,32]{0,1,2:T(8,128)} %add_bitcast_fusion.1) | data formatting | bytes 7864320 | tf_op jit(solution)/shard_map/add | solution.py:38
  158.8 23.0 %reshape_reshape.10 = f32[1,160,3,128,16]{4,3,2,1,0:T(8,128)} reshape(f32[480,64,32]{2,1,0:T(8,128)} %copy.78) | data formatting | bytes 7864320 | tf_op jit(solution)/shard_map/reshape;reshape | solution.py:73
  181.8 23.0 %reshape_reshape.11 = f32[1,160,3,128,16]{4,3,2,1,0:T(8,128)} reshape(f32[480,64,32]{2,1,0:T(8,128)} %copy.81) | data formatting | bytes 7864320 | tf_op jit(solution)/shard_map/reshape;reshape | solution.py:74
  204.8 30.7 %multiply_convert_fusion.1 = (bf16[1,160,3,128,16]{4,3,2,1,0:T(8,128)(2,1)}, bf16[1,160,3,128,16]{4,3,2,1,0:T(8,128)(2,1)}) fusion(f32[1,160,3,128,16]{4,3,2,1,0:T(8,128)} %reshape_reshape.10, f32[160]{0:T(256)S(1)} %multiply_multiply_fusion, f32[1,160,3,128,16]{4,3,2,1,0:T(8,128)} %reshape_reshape.11), kind=kLoop, calls=%fused_computation.2 | loop fusion | flops 3932160 | bytes 11797120 | tf_op jit(solution)/shard_map/convert
  235.6 21.6 %maximum_bitcast_fusion = bf16[128,2,160,3,16]{4,0,3,2,1:T(8,128)(2,1)} fusion(bf16[1,160,3,128,16]{4,3,2,1,0:T(8,128)(2,1)} %get-tuple-element.18, bf16[1,160,3,128,16]{4,3,2,1,0:T(8,128)(2,1)} %get-tuple-element.17), kind=kLoop, calls=%fused_computation | loop fusion | flops 1966080 | bytes 7864320 | tf_op jit(solution)/shard_map/transpose | solution.py:86
  257.2 35.3 %copy.82 = bf16[128,2,160,3,16]{2,4,3,1,0:T(8,128)(2,1)} copy(bf16[128,2,160,3,16]{4,0,3,2,1:T(8,128)(2,1)} %maximum_bitcast_fusion) | data formatting | bytes 7864320 | tf_op jit(solution)/shard_map/transpose | solution.py:86
  292.5 127.0 %all_to_all.10 = bf16[128,2,160,3,16]{2,4,3,1,0:T(8,128)(2,1)S(1)} all-to-all(bf16[128,2,160,3,16]{2,4,3,1,0:T(8,128)(2,1)} %copy.82), channel_id=1, replica_groups=mesh['inp'=8,'wide'=16] {'wide','inp'}, dimensions={0} | all-to-all | bytes 7864320 | tf_op jit(solution)/shard_map/all_to_all | solution.py:87
  419.6 0.9 fusion.84
  420.4 2.0 copy.88
  422.4 3.1 copy.84
  425.6 0.3 copy.87
  425.9 3.1 copy.83
  429.0 6.3 squeeze.5
  435.2 4.0 copy.86
  439.2 4.4 copy.90
  443.6 6.2 squeeze.4
  449.9 4.0 copy.85
  453.9 2.5 copy.89
  456.4 1.9 neg.13
  458.3 16.6 %multiply_bitcast_fusion = f32[8,2,160,1280]{3,2,0,1:T(8,128)} fusion(bf16[1,8,160,768]{3,2,1,0:T(8,128)(2,1)S(1)} %neg.13, bf16[1,8,160,768]{3,2,1,0:T(8,128)(2,1)} %copy.90, bf16[1,8,160,768]{3,2,1,0:T(8,128)(2,1)} %copy.89, bf16[1280,768]{1,0:T(8,128)(2,1)} %copy.86, bf16[1280,768]{1,0:T(8,128)(2,1)} %copy.85), kind=kOutput, calls=%fused_computation.3 | convolution fusion | flops 10108928000 | bytes 22937600 | tf_op jit(solution)/shard_map/pjak,bk->jpab/dot_general | solution.py:97
  474.9 10.7 %copy.93 = f32[8,2,160,1280]{3,2,1,0:T(8,128)} copy(f32[8,2,160,1280]{3,2,0,1:T(8,128)} %multiply_bitcast_fusion) | data formatting | bytes 26214400 | tf_op jit(solution)/shard_map/mul | solution.py:97
  485.6 151.5 %all_to_all.11 = f32[8,2,160,1280]{3,2,1,0:T(8,128)} all-to-all(f32[8,2,160,1280]{3,2,1,0:T(8,128)} %copy.93), channel_id=1, replica_groups=mesh['inp'=8,'wide'=16] {'inp'}, dimensions={0} | all-to-all | bytes 26214400 | tf_op jit(solution)/shard_map/all_to_all | solution.py:98
  637.1 11.0 %copy.94 = f32[2,8,160,1280]{3,2,1,0:T(8,128)} copy(f32[2,8,160,1280]{3,2,0,1:T(8,128)} %bitcast.65) | data formatting | bytes 26214400 | tf_op jit(solution)/shard_map/transpose | solution.py:99
  (2 shorter events, 0.0 us)
Async XLA Ops:
  7.0 4.7 copy-start.2
  7.0 4.7 copy-start.3
  7.5 7.8 %collective-permute-start = (bf16[160,3,4096]{2,0,1:T(8,128)(2,1)S(1)}, bf16[160,3,4096]{2,0,1:T(8,128)(2,1)}, u32[]{:S(2)}, u32[]{:S(2)}) collective-permute-start(bf16[160,3,4096]{2,0,1:T(8,128)(2,1)S(1)} %pad_maximum_fusion), channel_id=1, source_target_pairs={{0,1},{1,2},{2,3},{3,4},{4,5},{5,6},{6,7},{7,8},{8,9},{9,10},{10,1... | collective-permute-start | bytes 11796488 | tf_op jit(solution)/shard_map/ppermute | solution.py:14
  47.3 11.8 %copy-start = (f32[480,32,128]{2,1,0:T(8,128)S(1)}, f32[480,32,128]{2,1,0:T(8,128)}, u32[]{:S(2)}) copy-start(f32[480,32,128]{2,1,0:T(8,128)} %reshape_reshape.9) | copy-start | bytes 23592964
  71.5 15.4 %copy-start.1 = (f32[480,32,128]{2,1,0:T(8,128)S(1)}, f32[480,32,128]{2,1,0:T(8,128)}, u32[]{:S(2)}) copy-start(f32[480,32,128]{2,1,0:T(8,128)} %get-tuple-element.6) | copy-start | bytes 23592964

commit v2 on v1

v2 whole, which is shorter than its diff:
```python
import math

import jax
import jax.numpy as jnp
from jax import lax
from jax.sharding import PartitionSpec as P

AVG = 16


def passed_along(value, axis, steps):
    count = lax.axis_size(axis)
    initial, last = (max(0, -steps), min(count, count - steps))
    return lax.ppermute(value, axis, [(source, source + steps) for source in range(initial, last)])


def phase_tables(rows_count, cols_count, modulus):
    first_index = jnp.arange(rows_count, dtype=jnp.int32)[:, None]
    second_index = jnp.arange(cols_count, dtype=jnp.int32)[None, :]
    angle = (first_index * second_index % modulus).astype(jnp.float32) * (2.0 * math.pi / modulus)
    return (jnp.cos(angle), jnp.sin(angle))


def filter_frames(voltages, prototype):
    members, width_all = voltages.shape
    taps_count, span_len = prototype.shape
    frames_own = width_all // span_len
    samples = [voltages[:, f * span_len : (f + 1) * span_len].astype(jnp.float32) for f in range(frames_own)]
    near = []
    for f in range(frames_own):
        total = prototype[0][None, :] * samples[f]
        for tap_index in range(1, min(f, taps_count - 1) + 1):
            total = total + prototype[tap_index][None, :] * samples[f - tap_index]
        near.append(total)
    edge_parts = []
    for frame_index in range(taps_count - 1):
        partial_sum = jnp.zeros((members, span_len), jnp.float32)
        for tap_index in range(frame_index + 1, taps_count):
            partial_sum = partial_sum + prototype[tap_index][None, :] * samples[frames_own + frame_index - tap_index]
        edge_parts.append(partial_sum)
    outgoing = jnp.stack(edge_parts).astype(jnp.bfloat16)
    incoming = passed_along(outgoing, "wide", 1).astype(jnp.float32)
    rows = [near[f] + incoming[f] if f < taps_count - 1 else near[f] for f in range(frames_own)]
    return jnp.stack(rows)


def channelize(voltages, prototype, input_gain, usable):
    members = voltages.shape[0]
    span_len = prototype.shape[1]
    channels = span_len // 2
    filtered = filter_frames(voltages, prototype)
    frames_own = filtered.shape[0]
    rows = frames_own * members
    inner_len = min(span_len, 128)
    outer_len = span_len // inner_len
    kept_count = channels // outer_len
    highest = lax.Precision.HIGHEST
    shaped = filtered.reshape(rows, outer_len, inner_len)
    cos_one, sin_one = phase_tables(outer_len, outer_len, outer_len)
    first = jnp.concatenate([cos_one, -sin_one], axis=0)
    stage = jnp.einsum("ka,ran->krn", first, shaped, precision=highest)
    stage_real, stage_imag = stage[:outer_len], stage[outer_len:]
    cos_two, sin_two = phase_tables(outer_len, inner_len, span_len)
    turned_real = stage_real * cos_two[:, None, :] + stage_imag * sin_two[:, None, :]
    turned_imag = stage_imag * cos_two[:, None, :] - stage_real * sin_two[:, None, :]
    turned = jnp.concatenate([turned_real, turned_imag], axis=2)
    cos_three, sin_three = phase_tables(kept_count, inner_len, inner_len)
    second = jnp.concatenate(
        [jnp.concatenate([cos_three, sin_three], axis=1), jnp.concatenate([-sin_three, cos_three], axis=1)], axis=0
    )
    out = jnp.einsum("mn,krn->mkr", second, turned, precision=highest)
    out = out.reshape(2, channels, frames_own, members)
    factor = input_gain * usable.astype(jnp.float32) / math.sqrt(span_len)
    return (out * factor).astype(jnp.bfloat16).reshape(2, channels, rows)


def shards(voltages, prototype, input_gain, usable):
    members = voltages.shape[0]
    spectra = channelize(voltages, prototype, input_gain, usable)
    _, channels, rows = spectra.shape
    frames_own = rows // members
    n_inp = lax.axis_size("inp")
    n_wide = lax.axis_size("wide")
    n_dev = n_inp * n_wide
    group_width = channels // n_dev
    chunks = spectra.reshape(2, n_dev, group_width, rows).transpose(1, 0, 2, 3)
    arrived = lax.all_to_all(chunks, ("wide", "inp"), 0, 0, tiled=True)
    arrived = arrived.reshape(n_wide, n_inp, 2, group_width, frames_own, members)
    depth = n_wide * group_width * frames_own
    every = arrived.transpose(2, 0, 3, 4, 1, 5).reshape(2, depth, n_inp * members)
    real_part, imag_part = every[0], every[1]
    left = jnp.stack(
        [jnp.concatenate([real_part, imag_part], axis=0), jnp.concatenate([imag_part, -real_part], axis=0)]
    )
    right = jnp.concatenate([real_part, imag_part], axis=0)
    normalize = 1.0 / math.sqrt(depth)
    left = left.reshape(2, 2 * depth, n_inp, members)
    products = jnp.einsum("pkja,kb->jpab", left, right, preferred_element_type=jnp.float32) * normalize
    spread = lax.all_to_all(products, "inp", 0, 0, tiled=True)
    return spread.transpose(1, 0, 2, 3)


def solution(mesh):
    return jax.shard_map(
        shards,
        mesh=mesh,
        in_specs=(P("inp", "wide"), P(), P("inp"), P("inp")),
        out_specs=P(None, "wide", "inp", None),
        check_vma=False,
    )
```

time: 656 us -> 465 us (0.71)
  local copies, waits for them, and re-layouts: 190 us -> 85.9 us
  matrix products: 107 us -> 50.8 us
  blocking collectives: 279 us -> 258 us
  other arithmetic: 65.6 us -> 58.5 us
    dot_general x7 -> x2, matrix products: 107 us -> 37.9 us  [the longest x1 24.8 us: channelize(): out = jnp.einsum('mn,krn->mkr', second, turned, precision=highest)]
    another operation x3 -> x0, local copies, waits for them, and re-layouts: 59.6 us -> none  [the longest x1 23 us: channelize(): real_out.reshape(members, frames_own, channels) * factor]
    transpose x1, local copies, waits for them, and re-layouts: 35.3 us -> 0.45 us  [shards(): chunks = spectra.reshape(2, n_dev, group_width, rows).transpose(1, 0, 2, 3)]
    add x2 -> x0, local copies, waits for them, and re-layouts: 23.3 us -> none  [the longest x1 12.7 us: channelize(): near_sum + incoming]
    all_to_all x1, blocking collectives: 127 us -> 104 us  [shards(): arrived = lax.all_to_all(chunks, ('wide', 'inp'), 0, 0, tiled=True)]
    reshape x1, local copies, waits for them, and re-layouts: 0.9 us -> 18.1 us  [shards(): arrived.reshape(n_wide, n_inp, 2, group_width, frames_own, members)]
    transpose x1, other arithmetic: 21.6 us -> 4.68 us  [shards(): chunks = spectra.reshape(2, n_dev, group_width, rows).transpose(1, 0, 2, 3)]
    another operation x3 -> x5, other arithmetic: 32.4 us -> 16.3 us  [the longest x2 6.67 us: filter_frames(): outgoing = jnp.stack(edge_parts).astype(jnp.bfloat16)]
where the time goes in v2:
time: 465 us; the launch traced here: 461 us
  blocking collectives  258 us (55%)
  local copies, waits for them, and re-layouts  85.9 us (18%)
  other arithmetic  58.5 us (13%)
  matrix products  50.8 us (11%)
    all_to_all x1, blocking collectives, shards(): spread = lax.all_to_all(products, 'inp', 0, 0, tiled=True)  153 us
    all_to_all x1, blocking collectives, shards(): arrived = lax.all_to_all(chunks, ('wide', 'inp'), 0, 0, tiled=True)  104 us
    dot_general x1, matrix products, channelize(): out = jnp.einsum('mn,krn->mkr', second, turned, precision=highest)  24.8 us
    reshape x1, local copies, waits for them, and re-layouts, shards(): arrived.reshape(n_wide, n_inp, 2, group_width, frames_own, members)  18.1 us
    slice x3, local copies, waits for them, and re-layouts, shards(): real_part, imag_part = (every[0], every[1])  17.3 us
    dot_general x1, matrix products, channelize(): stage = jnp.einsum('ka,ran->krn', first, shaped, precision=highest)  13 us
    unnamed x1, matrix products  12.9 us
    concatenate x1, other arithmetic, channelize(): turned = jnp.concatenate([turned_real, turned_imag], axis=2)  12.9 us
  transfers between devices with their start and end apart: 1, of which 1 were waited for; matrix products, arithmetic and copies ran while one was open for 0% of the time, Pallas kernels for 0%

profile of v2, /device:TPU:0, one launch (start us, length us, event | category | flops | bytes accessed | tf_op | source)
XLA Modules:
  0.0 460.5 jit_solution(9991381770741071063)
XLA Ops:
  0.0 1.1 fusion.53
  1.1 4.5 fusion.13
  5.6 0.0 copy-start.2
  5.6 0.0 copy-start.3
  5.7 2.2 pad_maximum_fusion.2
  7.8 3.1 collective-permute-start
  11.0 0.0 copy-done.2
  11.0 0.0 copy-done.3
  11.0 0.1 mul.315
  11.1 0.1 sine_negate_fusion
  11.2 0.1 fusion.46
  11.2 0.1 fusion.45
  11.4 0.1 fusion.41
  11.5 4.3 collective-permute-done
  15.8 3.1 convert_element_type.55
  18.9 4.2 fusion.10
  23.1 0.8 pad_maximum_fusion.1
  24.0 1.7 copy.32
  25.7 13.0 %fusion.34 = f32[64,480,128]{2,0,1:T(8,128)S(1)} fusion(f32[480,32,128]{2,1,0:T(8,128)S(1)} %bitcast.64, f32[32,32]{0,1:T(8,128)S(1)} %get-tuple-element.19, f32[32,32]{0,1:T(8,128)S(1)} %get-tuple-element.20), kind=kOutput, calls=%fused_computation.59 | convolution fusion | flops 1509951488 | bytes 23601152 | tf_op jit(solution)/shard_map/ka,ran->krn/dot_general | solution.py:61
  38.7 6.9 %multiply_add_fusion = (f32[32,480,128]{2,0,1:T(8,128)}, f32[32,480,128]{2,0,1:T(8,128)}) fusion(f32[64,480,128]{2,0,1:T(8,128)S(1)} %fusion.34, f32[32,128]{1,0:T(8,128)S(1)} %get-tuple-element.21, f32[32,128]{1,0:T(8,128)S(1)} %get-tuple-element.22), kind=kLoop, calls=%fused_computation.8 | loop fusion | flops 11796480 | bytes 31490048 | tf_op jit(solution)/shard_map/add | solution.py:64
  45.6 12.9 %pad_maximum_fusion = f32[32,480,256]{2,0,1:T(8,128)} fusion(f32[32,480,128]{2,0,1:T(8,128)} %get-tuple-element.6, f32[32,480,128]{2,0,1:T(8,128)} %get-tuple-element.5), kind=kLoop, calls=%fused_computation | loop fusion | flops 3932160 | bytes 31457280 | tf_op jit(solution)/shard_map/concatenate | solution.py:66
  58.5 24.8 %fusion = f32[128,32,480]{0,2,1:T(8,128)} fusion(f32[32,480,256]{2,0,1:T(8,128)} %pad_maximum_fusion, f32[64,128]{1,0:T(8,128)S(1)} %get-tuple-element.24, f32[64,128]{1,0:T(8,128)S(1)} %fusion.45, f32[64,128]{1,0:T(8,128)S(1)} %get-tuple-element.23), kind=kOutput, calls=%fused_computation.1 | convolution fusion | flops 6039896064 | bytes 23691264 | tf_op jit(solution)/shard_map/mn,krn->mkr/dot_general | solution.py:71
  83.3 10.3 %copy.20 = f32[128,32,480]{2,1,0:T(8,128)} copy(f32[128,32,480]{0,2,1:T(8,128)} %fusion) | data formatting | bytes 15728640 | tf_op jit(solution)/shard_map/mn,krn->mkr/dot_general | solution.py:71
  93.5 4.7 %fusion.2 = bf16[128,2,16,480]{3,2,0,1:T(8,128)(2,1)S(1)} fusion(f32[2,128,16,480]{3,2,1,0:T(8,128)} %bitcast.67, f32[480]{0:T(512)S(1)} %mul.315), kind=kLoop, calls=%fused_computation.9 | loop fusion | flops 3932160 | bytes 11798400 | tf_op jit(solution)/shard_map/transpose | solution.py:86
  98.2 0.5 copy.21
  98.7 104.1 %all_to_all.10 = bf16[128,2,16,480]{3,2,1,0:T(8,128)(2,1)} all-to-all(bf16[128,2,16,480]{3,2,1,0:T(8,128)(2,1)S(1)} %copy.21), channel_id=1, replica_groups=mesh['inp'=8,'wide'=16] {'wide','inp'}, dimensions={0} | all-to-all | bytes 7864320 | tf_op jit(solution)/shard_map/all_to_all | solution.py:87
  202.8 18.1 %reshape.72 = bf16[16,8,2,16,3,160]{5,4,3,2,1,0:T(4,128)(2,1)} reshape(bf16[128,2,16,480]{3,2,1,0:T(8,128)(2,1)} %all_to_all.10) | data formatting | bytes 7864320 | tf_op jit(solution)/shard_map/reshape | solution.py:88
  220.9 8.0 %fusion.52 = (bf16[1,16,16,3,8,160]{5,3,2,0,4,1:T(4,128)(2,1)}, bf16[1,16,16,3,8,160]{5,3,2,0,4,1:T(4,128)(2,1)S(1)}) fusion(bf16[2,16,16,3,8,160]{5,3,2,0,4,1:T(4,128)(2,1)} %bitcast.66), kind=kLoop, calls=%fused_computation.79 | loop fusion | bytes 7864320 | tf_op jit(solution)/shard_map/slice | solution.py:91
  229.0 3.6 copy.22
  232.5 4.2 squeeze.18
  236.8 3.2 copy.26
  240.0 3.2 neg.16
  243.2 5.7 %copy.23 = bf16[1,16,16,3,8,160]{5,4,3,2,1,0:T(8,128)(2,1)S(1)} copy(bf16[1,16,16,3,8,160]{5,3,2,0,4,1:T(4,128)(2,1)} %get-tuple-element.10) | data formatting | bytes 3932160 | tf_op jit(solution)/shard_map/slice | solution.py:91
  248.9 4.2 squeeze.19
  253.1 3.5 copy.27
  256.6 0.0 copy-start
  256.6 0.0 copy-start.1
  256.6 4.7 %maximum_maximum_fusion = bf16[2,1536,8,160]{1,3,2,0:T(8,128)(2,1)S(1)} fusion(bf16[1,768,8,160]{1,3,2,0:T(8,128)(2,1)} %neg.16, bf16[1,768,8,160]{1,3,2,0:T(8,128)(2,1)} %copy.27, bf16[1,768,8,160]{1,3,2,0:T(8,128)(2,1)} %copy.26), kind=kLoop, calls=%fused_computation.6 | loop fusion | flops 31457280 | bytes 13762560 | tf_op jit(solution)/shard_map/stack | solution.py:92
  261.3 0.0 copy-done
  261.3 0.0 copy-done.1
  261.3 12.9 %fusion.3 = f32[1280,2560]{0,1} fusion(bf16[1536,2560]{0,1:T(8,128)(2,1)S(1)} %bitcast.72, bf16[768,1280]{1,0:T(8,128)(2,1)S(1)} %copy-done.1, bf16[768,1280]{1,0:T(8,128)(2,1)S(1)} %copy-done), kind=kOutput, calls=%fused_computation.11 | convolution fusion | flops 10074193920 | bytes 24903680
  274.2 11.0 %multiply_bitcast_fusion = f32[8,2,160,1280]{3,2,0,1:T(8,128)} fusion(f32[1280,2,8,160]{0,3,2,1:T(8,128)} %bitcast.71), kind=kLoop, calls=%fused_computation.3 | loop fusion | flops 3276800 | bytes 26214400 | tf_op jit(solution)/shard_map/mul | solution.py:98
  285.2 10.7 %copy.30 = f32[8,2,160,1280]{3,2,1,0:T(8,128)} copy(f32[8,2,160,1280]{3,2,0,1:T(8,128)} %multiply_bitcast_fusion) | data formatting | bytes 26214400 | tf_op jit(solution)/shard_map/mul | solution.py:98
  295.9 153.4 %all_to_all.11 = f32[8,2,160,1280]{3,2,1,0:T(8,128)} all-to-all(f32[8,2,160,1280]{3,2,1,0:T(8,128)} %copy.30), channel_id=1, replica_groups=mesh['inp'=8,'wide'=16] {'inp'}, dimensions={0} | all-to-all | bytes 26214400 | tf_op jit(solution)/shard_map/all_to_all | solution.py:99
  449.3 11.0 %copy.31 = f32[2,8,160,1280]{3,2,1,0:T(8,128)} copy(f32[2,8,160,1280]{3,2,0,1:T(8,128)} %bitcast.65) | data formatting | bytes 26214400 | tf_op jit(solution)/shard_map/transpose | solution.py:100
  (2 shorter events, 0.0 us)
Async XLA Ops:
  5.6 5.3 %copy-start.2 = (f32[160]{0:T(256)S(1)}, f32[160]{0:T(256)}, u32[]{:S(2)}) copy-start(f32[160]{0:T(256)} %param.6) | copy-start | bytes 1924
  5.6 5.3 %copy-start.3 = (s32[160]{0:T(256)S(1)}, s32[160]{0:T(256)}, u32[]{:S(2)}) copy-start(s32[160]{0:T(256)} %param.7) | copy-start | bytes 1924
  7.8 8.0 %collective-permute-start = (bf16[3,160,4096]{2,1,0:T(8,128)(2,1)}, bf16[3,160,4096]{2,1,0:T(8,128)(2,1)}, u32[]{:S(2)}, u32[]{:S(2)}) collective-permute-start(bf16[3,160,4096]{2,1,0:T(8,128)(2,1)} %pad_maximum_fusion.2), channel_id=1, source_target_pairs={{0,1},{1,2},{2,3},{3,4},{4,5},{5,6},{6,7},{7,8},{8,9},{9,10},{10,1... | collective-permute-start | bytes 11796488 | tf_op jit(solution)/shard_map/ppermute | solution.py:14
  256.6 4.7 %copy-start = (bf16[768,1280]{1,0:T(8,128)(2,1)S(1)}, bf16[768,1280]{1,0:T(8,128)(2,1)}, u32[]{:S(2)}) copy-start(bf16[768,1280]{1,0:T(8,128)(2,1)} %squeeze.18) | copy-start | bytes 5898244
  256.6 4.7 %copy-start.1 = (bf16[768,1280]{1,0:T(8,128)(2,1)S(1)}, bf16[768,1280]{1,0:T(8,128)(2,1)}, u32[]{:S(2)}) copy-start(bf16[768,1280]{1,0:T(8,128)(2,1)} %squeeze.19) | copy-start | bytes 5898244

commit v3 on v2

--- a/solution.py
+++ b/solution.py
@@ -87,15 +87,13 @@
     arrived = lax.all_to_all(chunks, ("wide", "inp"), 0, 0, tiled=True)
     arrived = arrived.reshape(n_wide, n_inp, 2, group_width, frames_own, members)
     depth = n_wide * group_width * frames_own
-    every = arrived.transpose(2, 0, 3, 4, 1, 5).reshape(2, depth, n_inp * members)
+    every = arrived.transpose(2, 1, 5, 0, 3, 4).reshape(2, n_inp * members, depth)
     real_part, imag_part = every[0], every[1]
-    left = jnp.stack(
-        [jnp.concatenate([real_part, imag_part], axis=0), jnp.concatenate([imag_part, -real_part], axis=0)]
-    )
-    right = jnp.concatenate([real_part, imag_part], axis=0)
+    right = jnp.concatenate([real_part, imag_part], axis=1)
+    left = jnp.stack([right, jnp.concatenate([imag_part, -real_part], axis=1)])
     normalize = 1.0 / math.sqrt(depth)
-    left = left.reshape(2, 2 * depth, n_inp, members)
-    products = jnp.einsum("pkja,kb->jpab", left, right, preferred_element_type=jnp.float32) * normalize
+    left = left.reshape(2, n_inp, members, left.shape[-1]).transpose(1, 0, 2, 3)
+    products = jnp.einsum("jpak,bk->jpab", left, right, preferred_element_type=jnp.float32) * normalize
     spread = lax.all_to_all(products, "inp", 0, 0, tiled=True)
     return spread.transpose(1, 0, 2, 3)
 

time: 465 us -> 449 us (0.966)
  other arithmetic: 58.5 us -> 43 us
    dot_general x0 -> x1, matrix products: none -> 14 us  [shards(): jnp.einsum('jpak,bk->jpab', left, right, preferred_element_type=jnp.float32)]
    unnamed x1 -> x0, matrix products: 12.9 us -> none
    mul x1 -> x0, other arithmetic: 11 us -> none  [shards(): jnp.einsum('pkja,kb->jpab', left, right, preferred_element_type=jnp.float32)]
    mul x1 -> x0, local copies, waits for them, and re-layouts: 10.7 us -> none  [shards(): jnp.einsum('pkja,kb->jpab', left, right, preferred_element_type=jnp.float32)]
    squeeze x2 -> x4, local copies, waits for them, and re-layouts: 8.45 us -> 18.5 us  [shards(): real_part, imag_part = (every[0], every[1])]
    another operation x1 -> x0, other arithmetic: 4.65 us -> none  [shards(): jnp.stack([jnp.concatenate([real_part, imag_part], axis=0), jnp.concatena...]
where the time goes in v3:
time: 449 us; the launch traced here: 444 us
  blocking collectives  254 us (57%)
  local copies, waits for them, and re-layouts  86.9 us (19%)
  matrix products  51.8 us (12%)
  other arithmetic  43 us (10%)
    all_to_all x1, blocking collectives, shards(): spread = lax.all_to_all(products, 'inp', 0, 0, tiled=True)  150 us
    all_to_all x1, blocking collectives, shards(): arrived = lax.all_to_all(chunks, ('wide', 'inp'), 0, 0, tiled=True)  104 us
    dot_general x1, matrix products, channelize(): out = jnp.einsum('mn,krn->mkr', second, turned, precision=highest)  24.8 us
    slice x3, local copies, waits for them, and re-layouts, shards(): real_part, imag_part = (every[0], every[1])  19 us
    squeeze x4, local copies, waits for them, and re-layouts, shards(): real_part, imag_part = (every[0], every[1])  18.5 us
    reshape x1, local copies, waits for them, and re-layouts, shards(): arrived.reshape(n_wide, n_inp, 2, group_width, frames_own, members)  18.1 us
    dot_general x1, matrix products, shards(): jnp.einsum('jpak,bk->jpab', left, right, preferred_element_type=jnp.float32)  14 us
    dot_general x1, matrix products, channelize(): stage = jnp.einsum('ka,ran->krn', first, shaped, precision=highest)  13 us
  transfers between devices with their start and end apart: 1, of which 1 were waited for; matrix products, arithmetic and copies ran while one was open for 0% of the time, Pallas kernels for 0%

profile of v3, /device:TPU:0, one launch (start us, length us, event | category | flops | bytes accessed | tf_op | source)
XLA Modules:
  0.0 444.0 jit_solution(11693351342430133454)
XLA Ops:
  0.0 1.1 fusion.57
  1.1 4.5 %fusion.17 = (bf16[1,160,4096]{2,1,0:T(8,128)(2,1)S(1)}, bf16[1,160,4096]{2,1,0:T(8,128)(2,1)S(1)}, bf16[1,160,4096]{2,1,0:T(8,128)(2,1)S(1)}) fusion(s32[160,12288]{1,0:T(8,128)} %param.4, f32[4096]{0:T(1024)S(1)} %bitcast.81, f32[4096]{0:T(1024)S(1)} %bitcast.78, f32[4096]{0:T(1024)S(1)} %bitcast.76), kind=kLoop, calls=%fused_computation.32 | loop fusion | flops 9830400 | bytes 11845632 | tf_op jit(solution)/shard_map/stack | solution.py:41
  5.6 0.0 copy-start.1
  5.6 0.0 copy-start.2
  5.7 2.2 pad_maximum_fusion.2
  7.8 3.2 collective-permute-start
  11.0 0.0 copy-done.1
  11.0 0.0 copy-done.2
  11.0 0.1 mul.312
  11.1 0.1 sine_negate_fusion
  11.2 0.1 fusion.50
  11.2 0.1 fusion.49
  11.4 0.1 fusion.45
  11.5 4.3 collective-permute-done
  15.8 3.1 convert_element_type.55
  18.9 4.2 fusion.14
  23.1 0.8 pad_maximum_fusion.1
  24.0 1.7 copy.36
  25.7 13.0 %fusion.38 = f32[64,480,128]{2,0,1:T(8,128)S(1)} fusion(f32[480,32,128]{2,1,0:T(8,128)S(1)} %bitcast.69, f32[32,32]{0,1:T(8,128)S(1)} %get-tuple-element.19, f32[32,32]{0,1:T(8,128)S(1)} %get-tuple-element.20), kind=kOutput, calls=%fused_computation.64 | convolution fusion | flops 1509951488 | bytes 23601152 | tf_op jit(solution)/shard_map/ka,ran->krn/dot_general | solution.py:61
  38.7 6.9 %multiply_add_fusion = (f32[32,480,128]{2,0,1:T(8,128)}, f32[32,480,128]{2,0,1:T(8,128)}) fusion(f32[64,480,128]{2,0,1:T(8,128)S(1)} %fusion.38, f32[32,128]{1,0:T(8,128)S(1)} %get-tuple-element.21, f32[32,128]{1,0:T(8,128)S(1)} %get-tuple-element.22), kind=kLoop, calls=%fused_computation.14 | loop fusion | flops 11796480 | bytes 31490048 | tf_op jit(solution)/shard_map/add | solution.py:64
  45.6 12.9 %pad_maximum_fusion = f32[32,480,256]{2,0,1:T(8,128)} fusion(f32[32,480,128]{2,0,1:T(8,128)} %get-tuple-element.6, f32[32,480,128]{2,0,1:T(8,128)} %get-tuple-element.5), kind=kLoop, calls=%fused_computation | loop fusion | flops 3932160 | bytes 31457280 | tf_op jit(solution)/shard_map/concatenate | solution.py:66
  58.5 24.8 %fusion = f32[128,32,480]{0,2,1:T(8,128)} fusion(f32[32,480,256]{2,0,1:T(8,128)} %pad_maximum_fusion, f32[64,128]{1,0:T(8,128)S(1)} %get-tuple-element.24, f32[64,128]{1,0:T(8,128)S(1)} %fusion.49, f32[64,128]{1,0:T(8,128)S(1)} %get-tuple-element.23), kind=kOutput, calls=%fused_computation.1 | convolution fusion | flops 6039896064 | bytes 23691264 | tf_op jit(solution)/shard_map/mn,krn->mkr/dot_general | solution.py:71
  83.3 10.3 %copy.22 = f32[128,32,480]{2,1,0:T(8,128)} copy(f32[128,32,480]{0,2,1:T(8,128)} %fusion) | data formatting | bytes 15728640 | tf_op jit(solution)/shard_map/mn,krn->mkr/dot_general | solution.py:71
  93.6 4.7 %fusion.8 = bf16[128,2,16,480]{3,2,0,1:T(8,128)(2,1)S(1)} fusion(f32[2,128,16,480]{3,2,1,0:T(8,128)} %bitcast.72, f32[480]{0:T(512)S(1)} %mul.312), kind=kLoop, calls=%fused_computation.15 | loop fusion | flops 3932160 | bytes 11798400 | tf_op jit(solution)/shard_map/transpose | solution.py:86
  98.3 0.5 copy.23
  98.7 104.1 %all_to_all.10 = bf16[128,2,16,480]{3,2,1,0:T(8,128)(2,1)} all-to-all(bf16[128,2,16,480]{3,2,1,0:T(8,128)(2,1)S(1)} %copy.23), channel_id=1, replica_groups=mesh['inp'=8,'wide'=16] {'wide','inp'}, dimensions={0} | all-to-all | bytes 7864320 | tf_op jit(solution)/shard_map/all_to_all | solution.py:87
  202.8 18.1 %reshape.72 = bf16[16,8,2,16,3,160]{5,4,3,2,1,0:T(4,128)(2,1)} reshape(bf16[128,2,16,480]{3,2,1,0:T(8,128)(2,1)} %all_to_all.10) | data formatting | bytes 7864320 | tf_op jit(solution)/shard_map/reshape | solution.py:88
  221.0 8.0 %fusion.56 = (bf16[1,8,160,16,16,3]{2,5,4,0,1,3:T(4,128)(2,1)}, bf16[1,8,160,16,16,3]{2,5,4,0,1,3:T(4,128)(2,1)S(1)}) fusion(bf16[2,8,160,16,16,3]{2,5,4,0,1,3:T(4,128)(2,1)} %bitcast.71), kind=kLoop, calls=%fused_computation.84 | loop fusion | bytes 7864320 | tf_op jit(solution)/shard_map/slice | solution.py:91
  229.0 3.6 copy.24
  232.6 4.2 squeeze.18
  236.8 4.0 copy.32
  240.8 7.4 %copy.25 = bf16[1,8,160,16,16,3]{2,1,5,4,3,0:T(8,128)(2,1)} copy(bf16[1,8,160,16,16,3]{2,5,4,0,1,3:T(4,128)(2,1)} %get-tuple-element.10) | data formatting | bytes 3932160 | tf_op jit(solution)/shard_map/slice | solution.py:91
  248.2 6.2 %squeeze.19 = bf16[1280,768]{0,1:T(8,128)(2,1)} reshape(bf16[1,8,160,16,16,3]{2,1,5,4,3,0:T(8,128)(2,1)} %copy.25) | data formatting | bytes 3932160 | tf_op jit(solution)/shard_map/squeeze | solution.py:91
  254.4 4.0 copy.33
  258.5 3.5 copy.26
  262.0 0.0 copy-start
  262.0 3.3 neg.16
  265.3 0.0 copy-done
  265.3 3.2 copy.27
  268.6 14.0 %convolution_multiply_fusion = f32[8,2,160,1280]{3,2,1,0:T(8,128)S(1)} fusion(bf16[1,8,160,768]{3,2,0,1:T(8,128)(2,1)} %neg.16, bf16[1,8,160,768]{3,2,0,1:T(8,128)(2,1)} %copy.27, bf16[1,8,160,768]{3,2,0,1:T(8,128)(2,1)} %copy.26, bf16[1280,768]{1,0:T(8,128)(2,1)} %copy.33, bf16[1280,768]{1,0:T(8,128)(2,1)} %copy.32), kind=kOutput, calls=%fused_computation.3 | convolution fusion | flops 10108928000 | bytes 22937600 | tf_op jit(solution)/shard_map/jpak,bk->jpab/dot_general | solution.py:96
  282.5 150.3 %all_to_all.11 = f32[8,2,160,1280]{3,2,1,0:T(8,128)} all-to-all(f32[8,2,160,1280]{3,2,1,0:T(8,128)S(1)} %convolution_multiply_fusion), channel_id=1, replica_groups=mesh['inp'=8,'wide'=16] {'inp'}, dimensions={0} | all-to-all | bytes 26214400 | tf_op jit(solution)/shard_map/all_to_all | solution.py:97
  432.8 11.0 %copy.34 = f32[2,8,160,1280]{3,2,1,0:T(8,128)} copy(f32[2,8,160,1280]{3,2,0,1:T(8,128)} %bitcast.70) | data formatting | bytes 26214400 | tf_op jit(solution)/shard_map/transpose | solution.py:98
  (2 shorter events, 0.0 us)
Async XLA Ops:
  5.6 5.3 %copy-start.1 = (f32[160]{0:T(256)S(1)}, f32[160]{0:T(256)}, u32[]{:S(2)}) copy-start(f32[160]{0:T(256)} %param.6) | copy-start | bytes 1924
  5.6 5.3 %copy-start.2 = (s32[160]{0:T(256)S(1)}, s32[160]{0:T(256)}, u32[]{:S(2)}) copy-start(s32[160]{0:T(256)} %param.7) | copy-start | bytes 1924
  7.8 8.0 %collective-permute-start = (bf16[3,160,4096]{2,1,0:T(8,128)(2,1)}, bf16[3,160,4096]{2,1,0:T(8,128)(2,1)}, u32[]{:S(2)}, u32[]{:S(2)}) collective-permute-start(bf16[3,160,4096]{2,1,0:T(8,128)(2,1)} %pad_maximum_fusion.2), channel_id=1, source_target_pairs={{0,1},{1,2},{2,3},{3,4},{4,5},{5,6},{6,7},{7,8},{8,9},{9,10},{10,1... | collective-permute-start | bytes 11796488 | tf_op jit(solution)/shard_map/ppermute | solution.py:14
  262.0 3.3 copy-start

commit v4 on v3

--- a/solution.py
+++ b/solution.py
@@ -84,16 +84,16 @@
     n_dev = n_inp * n_wide
     group_width = channels // n_dev
     chunks = spectra.reshape(2, n_dev, group_width, rows).transpose(1, 0, 2, 3)
-    arrived = lax.all_to_all(chunks, ("wide", "inp"), 0, 0, tiled=True)
+    lane = 128
+    flat = chunks.reshape(n_dev, (2 * group_width * rows) // lane, lane)
+    arrived = lax.all_to_all(flat, ("wide", "inp"), 0, 0, tiled=True)
     arrived = arrived.reshape(n_wide, n_inp, 2, group_width, frames_own, members)
     depth = n_wide * group_width * frames_own
-    every = arrived.transpose(2, 1, 5, 0, 3, 4).reshape(2, n_inp * members, depth)
-    real_part, imag_part = every[0], every[1]
-    right = jnp.concatenate([real_part, imag_part], axis=1)
-    left = jnp.stack([right, jnp.concatenate([imag_part, -real_part], axis=1)])
+    both = arrived.transpose(1, 5, 2, 0, 3, 4).reshape(n_inp * members, 2 * depth)
+    turned = jnp.concatenate([both[:, depth:], -both[:, :depth]], axis=1)
     normalize = 1.0 / math.sqrt(depth)
-    left = left.reshape(2, n_inp, members, left.shape[-1]).transpose(1, 0, 2, 3)
-    products = jnp.einsum("jpak,bk->jpab", left, right, preferred_element_type=jnp.float32) * normalize
+    left = jnp.stack([both.reshape(n_inp, members, 2 * depth), turned.reshape(n_inp, members, 2 * depth)], axis=1)
+    products = jnp.einsum("jpak,bk->jpab", left, both, preferred_element_type=jnp.float32) * normalize
     spread = lax.all_to_all(products, "inp", 0, 0, tiled=True)
     return spread.transpose(1, 0, 2, 3)
 

time: 449 us -> 458 us (1.020)
  local copies, waits for them, and re-layouts: 86.9 us -> 95.2 us
    slice x3 -> x0, local copies, waits for them, and re-layouts: 19 us -> none  [shards(): real_part, imag_part = (every[0], every[1])]
    squeeze x4 -> x0, local copies, waits for them, and re-layouts: 18.5 us -> none  [shards(): real_part, imag_part = (every[0], every[1])]
    reshape x0 -> x2, local copies, waits for them, and re-layouts: none -> 17.4 us  [the longest x1 10.8 us: shards(): arrived.transpose(1, 5, 2, 0, 3, 4).reshape(n_inp * members, 2 * depth)]
    transpose x0 -> x1, local copies, waits for them, and re-layouts: none -> 13.3 us  [shards(): arrived.transpose(1, 5, 2, 0, 3, 4).reshape(n_inp * members, 2 * depth)]
    another operation x0 -> x1, local copies, waits for them, and re-layouts: none -> 8.48 us  [shards(): jnp.stack([both.reshape(n_inp, members, 2 * depth), turned.reshape(n_inp,...]
    transpose x1, local copies, waits for them, and re-layouts: 0.45 us -> 7.82 us  [shards(): chunks = spectra.reshape(2, n_dev, group_width, rows).transpose(1, 0, 2, 3)]
where the time goes in v4:
time: 458 us; the launch traced here: 453 us
  blocking collectives  252 us (55%)
  local copies, waits for them, and re-layouts  95.2 us (21%)
  matrix products  51.9 us (11%)
  other arithmetic  46.3 us (10%)
    all_to_all x1, blocking collectives, shards(): spread = lax.all_to_all(products, 'inp', 0, 0, tiled=True)  150 us
    all_to_all x1, blocking collectives, shards(): arrived = lax.all_to_all(flat, ('wide', 'inp'), 0, 0, tiled=True)  101 us
    dot_general x1, matrix products, channelize(): out = jnp.einsum('mn,krn->mkr', second, turned, precision=highest)  24.8 us
    reshape x1, local copies, waits for them, and re-layouts, shards(): arrived.reshape(n_wide, n_inp, 2, group_width, frames_own, members)  17.7 us
    dot_general x1, matrix products, shards(): jnp.einsum('jpak,bk->jpab', left, both, preferred_element_type=jnp.float32)  14.1 us
    transpose x1, local copies, waits for them, and re-layouts, shards(): arrived.transpose(1, 5, 2, 0, 3, 4).reshape(n_inp * members, 2 * depth)  13.3 us
    dot_general x1, matrix products, channelize(): stage = jnp.einsum('ka,ran->krn', first, shaped, precision=highest)  13 us
    concatenate x1, other arithmetic, channelize(): turned = jnp.concatenate([turned_real, turned_imag], axis=2)  12.9 us
  transfers between devices with their start and end apart: 1, of which 1 were waited for; matrix products, arithmetic and copies ran while one was open for 0% of the time, Pallas kernels for 0%

profile of v4, /device:TPU:0, one launch (start us, length us, event | category | flops | bytes accessed | tf_op | source)
XLA Modules:
  0.0 452.9 jit_solution(4965872705636352411)
XLA Ops:
  0.0 1.1 fusion.53
  1.1 4.5 fusion.13
  5.6 0.0 copy-start
  5.6 0.0 copy-start.1
  5.7 2.2 pad_maximum_fusion.2
  7.8 3.2 collective-permute-start
  11.0 0.0 copy-done
  11.0 0.0 copy-done.1
  11.0 0.1 mul.312
  11.1 0.1 sine_negate_fusion
  11.2 0.1 fusion.46
  11.3 0.1 fusion.45
  11.4 0.1 fusion.41
  11.6 4.3 collective-permute-done
  15.8 3.1 convert_element_type.55
  18.9 4.2 fusion.10
  23.1 0.8 pad_maximum_fusion.1
  24.0 1.7 copy.30
  25.7 13.0 %fusion.34 = f32[64,480,128]{2,0,1:T(8,128)S(1)} fusion(f32[480,32,128]{2,1,0:T(8,128)S(1)} %bitcast.59, f32[32,32]{0,1:T(8,128)S(1)} %get-tuple-element.19, f32[32,32]{0,1:T(8,128)S(1)} %get-tuple-element.20), kind=kOutput, calls=%fused_computation.60 | convolution fusion | flops 1509951488 | bytes 23601152 | tf_op jit(solution)/shard_map/ka,ran->krn/dot_general | solution.py:61
  38.7 6.9 %multiply_add_fusion = (f32[32,480,128]{2,0,1:T(8,128)}, f32[32,480,128]{2,0,1:T(8,128)}) fusion(f32[64,480,128]{2,0,1:T(8,128)S(1)} %fusion.34, f32[32,128]{1,0:T(8,128)S(1)} %get-tuple-element.21, f32[32,128]{1,0:T(8,128)S(1)} %get-tuple-element.22), kind=kLoop, calls=%fused_computation.10 | loop fusion | flops 11796480 | bytes 31490048 | tf_op jit(solution)/shard_map/add | solution.py:64
  45.6 12.9 %pad_maximum_fusion = f32[32,480,256]{2,0,1:T(8,128)} fusion(f32[32,480,128]{2,0,1:T(8,128)} %get-tuple-element.6, f32[32,480,128]{2,0,1:T(8,128)} %get-tuple-element.5), kind=kLoop, calls=%fused_computation | loop fusion | flops 3932160 | bytes 31457280 | tf_op jit(solution)/shard_map/concatenate | solution.py:66
  58.5 24.8 %fusion = f32[128,32,480]{0,2,1:T(8,128)} fusion(f32[32,480,256]{2,0,1:T(8,128)} %pad_maximum_fusion, f32[64,128]{1,0:T(8,128)S(1)} %get-tuple-element.24, f32[64,128]{1,0:T(8,128)S(1)} %fusion.45, f32[64,128]{1,0:T(8,128)S(1)} %get-tuple-element.23), kind=kOutput, calls=%fused_computation.1 | convolution fusion | flops 6039896064 | bytes 23691264 | tf_op jit(solution)/shard_map/mn,krn->mkr/dot_general | solution.py:71
  83.3 10.3 %copy.19 = f32[128,32,480]{2,1,0:T(8,128)} copy(f32[128,32,480]{0,2,1:T(8,128)} %fusion) | data formatting | bytes 15728640 | tf_op jit(solution)/shard_map/mn,krn->mkr/dot_general | solution.py:71
  93.5 6.6 %fusion.5 = bf16[128,2,16,480]{3,2,0,1:T(8,128)(2,1)} fusion(f32[2,128,16,480]{3,2,1,0:T(8,128)} %bitcast.63, f32[480]{0:T(512)S(1)} %mul.312), kind=kLoop, calls=%fused_computation.11 | loop fusion | flops 3932160 | bytes 11798400 | tf_op jit(solution)/shard_map/transpose | solution.py:86
  100.2 7.8 %copy.20 = bf16[128,2,16,480]{0,3,2,1:T(8,128)(2,1)} copy(bf16[128,2,16,480]{3,2,0,1:T(8,128)(2,1)} %fusion.5) | data formatting | bytes 7864320 | tf_op jit(solution)/shard_map/transpose | solution.py:86
  108.0 6.6 %copy.21 = bf16[128,120,128]{2,1,0:T(8,128)(2,1)} copy(bf16[128,120,128]{0,2,1:T(8,128)(2,1)} %bitcast.65) | data formatting | bytes 7864320 | tf_op jit(solution)/shard_map/reshape | solution.py:88
  114.5 101.5 %all_to_all.10 = bf16[128,120,128]{2,1,0:T(8,128)(2,1)} all-to-all(bf16[128,120,128]{2,1,0:T(8,128)(2,1)} %copy.21), channel_id=1, replica_groups=mesh['inp'=8,'wide'=16] {'wide','inp'}, dimensions={0} | all-to-all | bytes 7864320 | tf_op jit(solution)/shard_map/all_to_all | solution.py:89
  216.0 17.7 %reshape.55 = bf16[16,8,2,16,3,160]{5,4,3,2,1,0:T(4,128)(2,1)} reshape(bf16[128,120,128]{2,1,0:T(8,128)(2,1)} %all_to_all.10) | data formatting | bytes 7864320 | tf_op jit(solution)/shard_map/reshape | solution.py:90
  233.8 13.3 %copy.22 = bf16[8,160,2,16,16,3]{1,0,5,4,3,2:T(8,128)(2,1)} copy(bf16[8,160,2,16,16,3]{1,5,4,2,0,3:T(4,128)(2,1)} %bitcast.62) | data formatting | bytes 7864320 | tf_op jit(solution)/shard_map/transpose | solution.py:92
  247.1 10.8 %reshape.56 = bf16[1280,1536]{0,1:T(8,128)(2,1)} reshape(bf16[8,160,2,16,16,3]{1,0,5,4,3,2:T(8,128)(2,1)} %copy.22) | data formatting | bytes 7864320 | tf_op jit(solution)/shard_map/reshape | solution.py:92
  257.9 2.4 fusion.52
  260.3 2.2 pad_maximum_fusion.3
  262.6 6.3 %copy.24 = bf16[1280,1536]{1,0:T(8,128)(2,1)} copy(bf16[1280,1536]{0,1:T(8,128)(2,1)} %pad_maximum_fusion.3) | data formatting | bytes 7864320 | tf_op jit(solution)/shard_map/concatenate | solution.py:93
  268.8 8.5 %copy.25 = bf16[8,1,160,1536]{3,2,1,0:T(8,128)(2,1)} copy(bf16[8,1,160,1536]{2,0,3,1:T(8,128)(2,1)} %bitcast.60) | data formatting | bytes 7864320 | tf_op jit(solution)/shard_map/stack;reshape;reshape | solution.py:95
  277.3 14.1 %convolution_multiply_fusion = f32[8,2,160,1280]{3,2,1,0:T(8,128)S(1)} fusion(bf16[8,1,160,1536]{3,2,1,0:T(8,128)(2,1)} %bitcast.66, bf16[8,1,160,1536]{3,2,1,0:T(8,128)(2,1)} %copy.25, bf16[1280,1536]{0,1:T(8,128)(2,1)} %reshape.56), kind=kOutput, calls=%fused_computation.3 | convolution fusion | flops 10073538560 | bytes 24903680 | tf_op jit(solution)/shard_map/jpak,bk->jpab/dot_general | solution.py:96
  291.4 150.2 %all_to_all.11 = f32[8,2,160,1280]{3,2,1,0:T(8,128)} all-to-all(f32[8,2,160,1280]{3,2,1,0:T(8,128)S(1)} %convolution_multiply_fusion), channel_id=1, replica_groups=mesh['inp'=8,'wide'=16] {'inp'}, dimensions={0} | all-to-all | bytes 26214400 | tf_op jit(solution)/shard_map/all_to_all | solution.py:97
  441.7 11.0 %copy.27 = f32[2,8,160,1280]{3,2,1,0:T(8,128)} copy(f32[2,8,160,1280]{3,2,0,1:T(8,128)} %bitcast.61) | data formatting | bytes 26214400 | tf_op jit(solution)/shard_map/transpose | solution.py:98
  (2 shorter events, 0.0 us)
Async XLA Ops:
  5.6 5.3 %copy-start = (f32[160]{0:T(256)S(1)}, f32[160]{0:T(256)}, u32[]{:S(2)}) copy-start(f32[160]{0:T(256)} %param.6) | copy-start | bytes 1924
  5.6 5.3 %copy-start.1 = (s32[160]{0:T(256)S(1)}, s32[160]{0:T(256)}, u32[]{:S(2)}) copy-start(s32[160]{0:T(256)} %param.7) | copy-start | bytes 1924
  7.8 8.0 %collective-permute-start = (bf16[3,160,4096]{2,1,0:T(8,128)(2,1)}, bf16[3,160,4096]{2,1,0:T(8,128)(2,1)}, u32[]{:S(2)}, u32[]{:S(2)}) collective-permute-start(bf16[3,160,4096]{2,1,0:T(8,128)(2,1)} %pad_maximum_fusion.2), channel_id=1, source_target_pairs={{0,1},{1,2},{2,3},{3,4},{4,5},{5,6},{6,7},{7,8},{8,9},{9,10},{10,1... | collective-permute-start | bytes 11796488 | tf_op jit(solution)/shard_map/ppermute | solution.py:14

commit v5 on v3

--- a/solution.py
+++ b/solution.py
@@ -63,12 +63,12 @@
     cos_two, sin_two = phase_tables(outer_len, inner_len, span_len)
     turned_real = stage_real * cos_two[:, None, :] + stage_imag * sin_two[:, None, :]
     turned_imag = stage_imag * cos_two[:, None, :] - stage_real * sin_two[:, None, :]
-    turned = jnp.concatenate([turned_real, turned_imag], axis=2)
+    turned = jnp.stack([turned_real, turned_imag])
     cos_three, sin_three = phase_tables(kept_count, inner_len, inner_len)
-    second = jnp.concatenate(
-        [jnp.concatenate([cos_three, sin_three], axis=1), jnp.concatenate([-sin_three, cos_three], axis=1)], axis=0
+    second = jnp.stack(
+        [jnp.stack([cos_three, sin_three], axis=1), jnp.stack([-sin_three, cos_three], axis=1)]
     )
-    out = jnp.einsum("mn,krn->mkr", second, turned, precision=highest)
+    out = jnp.einsum("pmqn,qkrn->pmkr", second, turned, precision=highest)
     out = out.reshape(2, channels, frames_own, members)
     factor = input_gain * usable.astype(jnp.float32) / math.sqrt(span_len)
     return (out * factor).astype(jnp.bfloat16).reshape(2, channels, rows)

time: 449 us -> 440 us (0.980)
  local copies, waits for them, and re-layouts: 86.9 us -> 81.5 us
    another operation x0 -> x3, other arithmetic: none -> 19.8 us  [the longest x2 19.7 us: channelize(): turned = jnp.stack([turned_real, turned_imag])]
    concatenate x1 -> x0, other arithmetic: 12.9 us -> none  [channelize(): turned = jnp.concatenate([turned_real, turned_imag], axis=2)]
    add x1 -> x0, other arithmetic: 6.86 us -> none  [channelize(): stage_real * cos_two[:, None, :] + stage_imag * sin_two[:, None, :]]
    dot_general x1, local copies, waits for them, and re-layouts: 10.3 us -> 4.86 us  [channelize(): out = jnp.einsum('pmqn,qkrn->pmkr', second, turned, precision=highest)]
where the time goes in v5:
time: 440 us; the launch traced here: 436 us
  blocking collectives  255 us (58%)
  local copies, waits for them, and re-layouts  81.5 us (19%)
  matrix products  51.8 us (12%)
  other arithmetic  40 us (9%)
    all_to_all x1, blocking collectives, shards(): spread = lax.all_to_all(products, 'inp', 0, 0, tiled=True)  150 us
    all_to_all x1, blocking collectives, shards(): arrived = lax.all_to_all(chunks, ('wide', 'inp'), 0, 0, tiled=True)  104 us
    dot_general x1, matrix products, channelize(): out = jnp.einsum('pmqn,qkrn->pmkr', second, turned, precision=highest)  25.1 us
    another operation x2, other arithmetic, channelize(): turned = jnp.stack([turned_real, turned_imag])  19.7 us
    slice x3, local copies, waits for them, and re-layouts, shards(): real_part, imag_part = (every[0], every[1])  19 us
    squeeze x4, local copies, waits for them, and re-layouts, shards(): real_part, imag_part = (every[0], every[1])  18.5 us
    reshape x1, local copies, waits for them, and re-layouts, shards(): arrived.reshape(n_wide, n_inp, 2, group_width, frames_own, members)  18.1 us
    dot_general x1, matrix products, shards(): jnp.einsum('jpak,bk->jpab', left, right, preferred_element_type=jnp.float32)  14 us
  transfers between devices with their start and end apart: 1, of which 1 were waited for; matrix products, arithmetic and copies ran while one was open for 0% of the time, Pallas kernels for 0%

profile of v5, /device:TPU:0, one launch (start us, length us, event | category | flops | bytes accessed | tf_op | source)
XLA Modules:
  0.0 435.7 jit_solution(1250427170577599779)
XLA Ops:
  0.0 1.1 fusion.57
  1.1 4.5 %fusion.21 = (bf16[1,160,4096]{2,1,0:T(8,128)(2,1)S(1)}, bf16[1,160,4096]{2,1,0:T(8,128)(2,1)S(1)}, bf16[1,160,4096]{2,1,0:T(8,128)(2,1)S(1)}) fusion(s32[160,12288]{1,0:T(8,128)} %param.4, f32[4096]{0:T(1024)S(1)} %bitcast.99, f32[4096]{0:T(1024)S(1)} %bitcast.96, f32[4096]{0:T(1024)S(1)} %bitcast.94), kind=kLoop, calls=%fused_computation.34 | loop fusion | flops 9830400 | bytes 11845632 | tf_op jit(solution)/shard_map/stack | solution.py:41
  5.6 0.0 copy-start.1
  5.6 0.0 copy-start.2
  5.6 2.2 pad_maximum_fusion.2
  7.8 3.1 collective-permute-start
  11.0 0.0 copy-done.1
  11.0 0.0 copy-done.2
  11.0 0.1 mul.342
  11.1 0.1 sine_negate_fusion
  11.1 0.1 fusion.50
  11.2 0.1 fusion.49
  11.4 0.1 fusion.45
  11.6 4.3 collective-permute-done
  15.8 3.1 convert_element_type.70
  18.9 4.2 fusion.18
  23.1 1.1 pad_maximum_fusion.1
  24.3 1.7 copy.38
  26.0 12.7 %fusion.38 = f32[64,480,128]{2,0,1:T(8,128)S(1)} fusion(f32[480,32,128]{2,1,0:T(8,128)S(1)} %bitcast.87, f32[32,32]{0,1:T(8,128)S(1)} %get-tuple-element.21, f32[32,32]{0,1:T(8,128)S(1)} %get-tuple-element.22), kind=kOutput, calls=%fused_computation.64 | convolution fusion | flops 1509951488 | bytes 23601152 | tf_op jit(solution)/shard_map/ka,ran->krn/dot_general | solution.py:61
  38.7 6.9 %add_bitcast_fusion = (f32[1,32,480,128]{3,1,2,0:T(8,128)}, f32[1,32,480,128]{3,1,2,0:T(8,128)}) fusion(f32[64,480,128]{2,0,1:T(8,128)S(1)} %fusion.38, f32[32,128]{1,0:T(8,128)S(1)} %get-tuple-element.23, f32[32,128]{1,0:T(8,128)S(1)} %get-tuple-element.24), kind=kLoop, calls=%fused_computation.15 | loop fusion | flops 11796480 | bytes 31490048 | tf_op jit(solution)/shard_map/stack | solution.py:66
  45.6 12.9 %pad_maximum_fusion = f32[2,32,480,128]{3,1,2,0:T(8,128)} fusion(f32[1,32,480,128]{3,1,2,0:T(8,128)} %get-tuple-element.6, f32[1,32,480,128]{3,1,2,0:T(8,128)} %get-tuple-element.5), kind=kLoop, calls=%fused_computation | loop fusion | flops 3932160 | bytes 31457280 | tf_op jit(solution)/shard_map/stack | solution.py:66
  58.5 25.1 %fusion.12 = f32[2,64,32,480]{3,1,2,0:T(8,128)S(1)} fusion(f32[2,32,480,128]{3,1,2,0:T(8,128)} %pad_maximum_fusion, f32[1,64,2,128]{3,1,2,0:T(8,128)S(1)} %get-tuple-element.20, f32[1,64,2,128]{3,1,2,0:T(8,128)S(1)} %get-tuple-element.19), kind=kOutput, calls=%fused_computation.21 | convolution fusion | flops 6039830528 | bytes 23724032 | tf_op jit(solution)/shard_map/pmqn,qkrn->pmkr/dot_general | solution.py:71
  83.6 4.9 %copy.22 = f32[2,64,32,480]{3,2,1,0:T(8,128)S(1)} copy(f32[2,64,32,480]{3,1,2,0:T(8,128)S(1)} %fusion.12) | data formatting | bytes 15728640 | tf_op jit(solution)/shard_map/pmqn,qkrn->pmkr/dot_general | solution.py:71
  88.5 1.4 fusion.9
  89.9 0.5 copy.23
  90.3 104.3 %all_to_all.10 = bf16[128,2,16,480]{3,2,1,0:T(8,128)(2,1)} all-to-all(bf16[128,2,16,480]{3,2,1,0:T(8,128)(2,1)S(1)} %copy.23), channel_id=1, replica_groups=mesh['inp'=8,'wide'=16] {'wide','inp'}, dimensions={0} | all-to-all | bytes 7864320 | tf_op jit(solution)/shard_map/all_to_all | solution.py:87
  194.7 18.1 %reshape.147 = bf16[16,8,2,16,3,160]{5,4,3,2,1,0:T(4,128)(2,1)} reshape(bf16[128,2,16,480]{3,2,1,0:T(8,128)(2,1)} %all_to_all.10) | data formatting | bytes 7864320 | tf_op jit(solution)/shard_map/reshape | solution.py:88
  212.8 8.0 %fusion.56 = (bf16[1,8,160,16,16,3]{2,5,4,0,1,3:T(4,128)(2,1)}, bf16[1,8,160,16,16,3]{2,5,4,0,1,3:T(4,128)(2,1)S(1)}) fusion(bf16[2,8,160,16,16,3]{2,5,4,0,1,3:T(4,128)(2,1)} %bitcast.89), kind=kLoop, calls=%fused_computation.84 | loop fusion | bytes 7864320 | tf_op jit(solution)/shard_map/slice | solution.py:91
  220.8 3.6 copy.24
  224.4 4.2 squeeze.18
  228.6 4.0 copy.32
  232.6 7.4 %copy.25 = bf16[1,8,160,16,16,3]{2,1,5,4,3,0:T(8,128)(2,1)} copy(bf16[1,8,160,16,16,3]{2,5,4,0,1,3:T(4,128)(2,1)} %get-tuple-element.10) | data formatting | bytes 3932160 | tf_op jit(solution)/shard_map/slice | solution.py:91
  240.0 6.3 %squeeze.19 = bf16[1280,768]{0,1:T(8,128)(2,1)} reshape(bf16[1,8,160,16,16,3]{2,1,5,4,3,0:T(8,128)(2,1)} %copy.25) | data formatting | bytes 3932160 | tf_op jit(solution)/shard_map/squeeze | solution.py:91
  246.3 4.0 copy.33
  250.3 3.5 copy.26
  253.8 0.0 copy-start
  253.8 3.3 neg.23
  257.1 0.0 copy-done
  257.1 3.2 copy.27
  260.3 14.0 %convolution_multiply_fusion = f32[8,2,160,1280]{3,2,1,0:T(8,128)S(1)} fusion(bf16[1,8,160,768]{3,2,0,1:T(8,128)(2,1)} %neg.23, bf16[1,8,160,768]{3,2,0,1:T(8,128)(2,1)} %copy.27, bf16[1,8,160,768]{3,2,0,1:T(8,128)(2,1)} %copy.26, bf16[1280,768]{1,0:T(8,128)(2,1)} %copy.33, bf16[1280,768]{1,0:T(8,128)(2,1)} %copy.32), kind=kOutput, calls=%fused_computation.4 | convolution fusion | flops 10108928000 | bytes 22937600 | tf_op jit(solution)/shard_map/jpak,bk->jpab/dot_general | solution.py:96
  274.3 150.3 %all_to_all.11 = f32[8,2,160,1280]{3,2,1,0:T(8,128)} all-to-all(f32[8,2,160,1280]{3,2,1,0:T(8,128)S(1)} %convolution_multiply_fusion), channel_id=1, replica_groups=mesh['inp'=8,'wide'=16] {'inp'}, dimensions={0} | all-to-all | bytes 26214400 | tf_op jit(solution)/shard_map/all_to_all | solution.py:97
  424.6 11.0 %copy.34 = f32[2,8,160,1280]{3,2,1,0:T(8,128)} copy(f32[2,8,160,1280]{3,2,0,1:T(8,128)} %bitcast.88) | data formatting | bytes 26214400 | tf_op jit(solution)/shard_map/transpose | solution.py:98
  (3 shorter events, 0.0 us)
Async XLA Ops:
  5.6 5.3 %copy-start.1 = (f32[160]{0:T(256)S(1)}, f32[160]{0:T(256)}, u32[]{:S(2)}) copy-start(f32[160]{0:T(256)} %param.6) | copy-start | bytes 1924
  5.6 5.3 %copy-start.2 = (s32[160]{0:T(256)S(1)}, s32[160]{0:T(256)}, u32[]{:S(2)}) copy-start(s32[160]{0:T(256)} %param.7) | copy-start | bytes 1924
  7.8 8.0 %collective-permute-start = (bf16[3,160,4096]{2,1,0:T(8,128)(2,1)}, bf16[3,160,4096]{2,1,0:T(8,128)(2,1)}, u32[]{:S(2)}, u32[]{:S(2)}) collective-permute-start(bf16[3,160,4096]{2,1,0:T(8,128)(2,1)} %pad_maximum_fusion.2), channel_id=1, source_target_pairs={{0,1},{1,2},{2,3},{3,4},{4,5},{5,6},{6,7},{7,8},{8,9},{9,10},{10,1... | collective-permute-start | bytes 11796488 | tf_op jit(solution)/shard_map/ppermute | solution.py:14
  253.8 3.3 copy-start
